TPU v7x, 256 devices: a whole 4x4x8 slice. The times are simulated.
256 devices in a mesh: row: 16 (over z_hi, y, core), col: 16 (over x, z_lo).
Axes of the slice: x: 4, y: 4, z: 8 (z_hi: 2, z_lo: 4; z = z_hi * 4 + z_lo), core: 2. Of those that a mesh axis runs over, the one named last changes fastest.
Arguments:
- coefficients: float32 [8192, 8192], P('row', 'col'), may hold values from -6 to 6
- alpha_pattern: int32 [16, 10], P('row'), may hold values from 0 to 15, all different within a row
- alpha_count: int32 [16], P('row'), may hold values from 1 to 10
- alpha_blocks: bfloat16 [16, 10, 512, 512], P('row'), may hold values from -0.078125 to 0.078125
- beta_pattern: int32 [16, 10], P('col'), may hold values from 0 to 15, all different within a row
- beta_count: int32 [16], P('col'), may hold values from 1 to 10
- beta_blocks: bfloat16 [16, 10, 512, 512], P('col'), may hold values from -0.078125 to 0.078125
Outputs:
- sigma: float32 [8192, 8192], P('row', 'col')
Inputs may be any that keep to these rules, and one draw needn't show every extreme that they name: `alpha_pattern`: each row lists 10 different blocks, and every block stands in some row. `beta_pattern`: each row lists 10 different blocks, and every block stands in some row.
All inputs are finite; a program needn't handle non-finite values.
Results may differ from a plain program's by a relative error of at most 0.0029.
Values may be sent and summed in bfloat16 or wider, within the bound.
No kernel may reach another device: no remote copies, remote signals or barrier semaphores. Data moves between devices by JAX's collectives and lax.ppermute only.
A program may use at most 128 MiB of HBM per device.

v0:
```python
import jax
import jax.numpy as jnp
from jax import lax
from jax.sharding import PartitionSpec as P


def slot_mask(count, slots):
    return lax.broadcasted_iota(jnp.int32, (count.shape[0], slots), 1) < count[:, None]


def body(
    coefficients, alpha_pattern, alpha_count, alpha_blocks, beta_pattern, beta_count, beta_blocks
):
    coeff_bf = coefficients.astype(jnp.bfloat16)
    tile_rows, tile_cols = coeff_bf.shape
    slots = alpha_blocks.shape[1]
    block = alpha_blocks.shape[2]
    strings = tile_rows * lax.axis_size("row")
    blocks_all = strings // block
    alpha_mask = slot_mask(alpha_count, slots).astype(jnp.bfloat16)
    beta_mask = slot_mask(beta_count, slots).astype(jnp.bfloat16)
    column_slab = lax.all_gather(coeff_bf, "row", axis=0, tiled=True)
    row_slab = lax.all_gather(coeff_bf, "col", axis=1, tiled=True)
    slab_blocks = column_slab.reshape(blocks_all, block, tile_cols)
    slab_cols = row_slab.reshape(tile_rows, blocks_all, block)
    weighted = alpha_blocks * alpha_mask[:, :, None, None]
    picked = slab_blocks[alpha_pattern]
    alpha_term = jnp.einsum("itab,itbc->iac", weighted, picked, preferred_element_type=jnp.float32)
    beta_weighted = beta_blocks * beta_mask[:, :, None, None]
    beta_picked = slab_cols[:, beta_pattern, :]
    beta_term = jnp.einsum(
        "abtk,btck->bac", beta_picked, beta_weighted, preferred_element_type=jnp.float32
    )
    alpha_term = alpha_term.reshape(tile_rows, tile_cols)
    beta_term = jnp.transpose(beta_term, (1, 0, 2)).reshape(tile_rows, tile_cols)
    return alpha_term + beta_term


def solution(mesh):
    placed = (
        P("row", "col"),
        P("row", None),
        P("row"),
        P("row", None, None, None),
        P("col", None),
        P("col"),
        P("col", None, None, None),
    )
    return jax.shard_map(
        body, mesh=mesh, in_specs=placed, out_specs=P("row", "col"), check_vma=False
    )
```

profile of v0, /device:TPU:1, one launch (start us, length us, event | category | flops | bytes accessed | tf_op | source)
XLA Modules:
  0.0 356.1 jit_solution(14214862564943844612)
XLA Ops:
  6.5 0.0 all-gather.5.cloned.1.call-start
  6.5 2.2 copy.10
  8.8 0.0 all-gather.5.cloned.1.call-update
  8.8 0.0 all-gather.3.cloned.1.call-start
  8.8 0.7 all-gather.3.cloned.1.call-update
  10.9 0.7 fusion.22
  11.5 0.7 fusion.23
  12.2 185.9 %all-gather.5.cloned.1.call-done = bf16[512,8192]{0,1:T(8,128)(2,1)} async-done(((bf16[512,512]{0,1:T(8,128)(2,1)}), bf16[512,8192]{0,1:T(8,128)(2,1)}) %all-gather.5.cloned.1.call-update) | async-done | bytes 8388624 | tf_op jit(solution)/shard_map/all_gather | solution.py:23
  198.1 12.3 %copy.12 = bf16[512,16,512]{2,0,1:T(8,128)(2,1)} copy(bf16[512,16,512]{0,2,1:T(8,128)(2,1)} %bitcast.37) | data formatting | bytes 16777216 | tf_op jit(solution)/shard_map/reshape | solution.py:25
  210.4 101.7 %all-gather.3.cloned.1.call-done = bf16[8192,512]{0,1:T(8,128)(2,1)} async-done(((bf16[512,512]{0,1:T(8,128)(2,1)}), bf16[8192,512]{0,1:T(8,128)(2,1)}) %all-gather.3.cloned.1.call-update) | async-done | bytes 8388624 | tf_op jit(solution)/shard_map/all_gather | solution.py:22
  312.1 11.9 %copy.11 = bf16[8192,512]{1,0:T(8,128)(2,1)} copy(bf16[8192,512]{0,1:T(8,128)(2,1)} %all-gather.3.cloned.1.call-done) | data formatting | bytes 16777216 | tf_op jit(solution)/shard_map/all_gather | solution.py:22
  324.0 7.2 %gather_fusion = bf16[10,512,512]{2,1,0:T(8,128)(2,1)} fusion(bf16[16,512,512]{2,1,0:T(8,128)(2,1)} %bitcast.36, s32[1024]{0:T(1024)S(1)} %pad_clamp_fusion.1), kind=kCustom, calls=%fused_computation | custom fusion | bytes 10485800 | tf_op jit(solution)/shard_map/gather | solution.py:27
  331.2 0.0 slice-start
  331.2 7.3 %gather_fusion.1 = bf16[10,512,512]{2,1,0:T(8,128)(2,1)} fusion(bf16[512,16,512]{2,0,1:T(8,128)(2,1)} %copy.12, s32[1024]{0:T(1024)S(1)} %pad_clamp_fusion), kind=kCustom, calls=%fused_computation.1 | custom fusion | bytes 10485800 | tf_op jit(solution)/shard_map/gather | solution.py:30
  338.5 0.0 copy-start
  338.5 0.0 slice-start.1
  338.6 6.6 %fusion.9 = f32[512,512]{1,0:T(8,128)S(1)} fusion(bf16[10,512,512]{2,1,0:T(8,128)(2,1)} %gather_fusion, bf16[1,10,512,512]{3,2,1,0:T(8,128)(2,1)} %param.10, bf16[10]{0:T(256)(128)(2,1)S(1)} %compare_convert_fusion.1), kind=kOutput, calls=%fused_computation.11 | convolution fusion | flops 2686976000 | bytes 11534356 | tf_op jit(solution)/shard_map/itab,itbc->iac/dot_general | solution.py:28
  345.1 0.0 slice-done
  345.1 0.0 copy-done
  345.1 0.2 slice-done.1
  345.3 4.0 %fusion.17 = f32[512,512]{1,0:T(8,128)} fusion(f32[512,512]{1,0:T(8,128)S(1)} %fusion.9, bf16[1,10,512,512]{3,2,1,0:T(8,128)(2,1)S(1)} %bitcast.39, bf16[10]{0:T(256)(128)(2,1)S(1)} %compare_convert_fusion, bf16[10,512,512]{2,1,0:T(8,128)(2,1)S(1)} %copy-done), kind=kOutput, calls=%fused_computation.13 | convolution fusion | flops 2687238144 | bytes 12582932 | tf_op jit(solution)/shard_map/abtk,btck->bac/dot_general | solution.py:31
  (5 shorter events, 0.0 us)
Async XLA Ops:
  6.5 191.5 %all-gather.5.cloned.1.call-start = ((), (), s32[]{:S(2)}) async-start(), calls=%async_computation.1 | async-start | bytes 8912896 | tf_op jit(solution)/shard_map/all_gather | solution.py:23
  8.8 303.3 %all-gather.3.cloned.1.call-start = ((), (), s32[]{:S(2)}) async-start(), calls=%async_computation | async-start | bytes 8912896 | tf_op jit(solution)/shard_map/all_gather | solution.py:22
  331.2 13.9 %slice-start = ((s8[5242880]{0:T(1024)(128)(4,1)}), s8[1048576]{0:T(1024)(128)(4,1)S(1)}, s32[]{:S(2)}) async-start(s8[5242880]{0:T(1024)(128)(4,1)} %bitcast.38), calls=%async_computation.2 | async-start | bytes 2097152
  338.5 6.6 %copy-start = (bf16[10,512,512]{2,1,0:T(8,128)(2,1)S(1)}, bf16[10,512,512]{2,1,0:T(8,128)(2,1)}, u32[]{:S(2)}) copy-start(bf16[10,512,512]{2,1,0:T(8,128)(2,1)} %gather_fusion.1) | copy-start | bytes 15728644
  338.5 6.8 %slice-start.1 = ((s8[5242880]{0:T(1024)(128)(4,1)}), s8[4194304]{0:T(1024)(128)(4,1)S(1)}, s32[]{:S(2)}) async-start(s8[5242880]{0:T(1024)(128)(4,1)} %bitcast.38), calls=%async_computation.3 | async-start | bytes 8388608
Sparse Core Ops, SparseCore 0:
  9.1 188.8 all-gather.4
  200.6 111.4 all-gather.2
where the time goes:
time: 357 us; the launch traced here: 356 us
  waiting for transfers between devices  288 us (81%)
  local copies, waits for them, and re-layouts  41.2 us (12%)
  between operations  14.7 us (4%)
  matrix products  10.5 us (3%)
    all_gather x1, waiting for transfers between devices, body(): row_slab = lax.all_gather(coeff_bf, 'col', axis=1, tiled=True)  186 us
    all_gather x1, waiting for transfers between devices, body(): column_slab = lax.all_gather(coeff_bf, 'row', axis=0, tiled=True)  102 us
    reshape x1, local copies, waits for them, and re-layouts, body(): slab_cols = row_slab.reshape(tile_rows, blocks_all, block)  12.3 us
    all_gather x1, local copies, waits for them, and re-layouts, body(): column_slab = lax.all_gather(coeff_bf, 'row', axis=0, tiled=True)  11.9 us
    gather x1, local copies, waits for them, and re-layouts, body(): beta_picked = slab_cols[:, beta_pattern, :]  7.34 us
    gather x1, local copies, waits for them, and re-layouts, body(): picked = slab_blocks[alpha_pattern]  7.22 us
  transfers between devices with their start and end apart: 2, of which 2 were waited for; matrix products, arithmetic and copies ran while one was open for 4% of the time, Pallas kernels for 0%

commit v1 on v0

--- a/solution.py
+++ b/solution.py
@@ -20,7 +20,15 @@
     alpha_mask = slot_mask(alpha_count, slots).astype(jnp.bfloat16)
     beta_mask = slot_mask(beta_count, slots).astype(jnp.bfloat16)
     column_slab = lax.all_gather(coeff_bf, "row", axis=0, tiled=True)
-    row_slab = lax.all_gather(coeff_bf, "col", axis=1, tiled=True)
+    row_slab = jnp.concatenate(
+        lax.all_to_all(
+            jnp.stack([coeff_bf for _ in range(lax.axis_size("col"))], axis=0),
+            split_axis=0,
+            concat_axis=0,
+            axis_name="col",
+        ),
+        1,
+    )
     slab_blocks = column_slab.reshape(blocks_all, block, tile_cols)
     slab_cols = row_slab.reshape(tile_rows, blocks_all, block)
     weighted = alpha_blocks * alpha_mask[:, :, None, None]

time: 357 us -> 289 us (0.81)
  waiting for transfers between devices: 288 us -> 232 us
  local copies, waits for them, and re-layouts: 41.2 us -> 20 us
  starting transfers between devices: 0.04 us -> 9.19 us
    all_gather x1 -> x0, waiting for transfers between devices: 186 us -> none  [body(): row_slab = lax.all_gather(coeff_bf, 'col', axis=1, tiled=True)]
    all_to_all x0 -> x1, waiting for transfers between devices: none -> 123 us  [body(): lax.all_to_all(jnp.stack([coeff_bf for _ in range(lax.axis_size('col'))],...]
    reshape x1 -> x0, local copies, waits for them, and re-layouts: 12.3 us -> none  [body(): slab_cols = row_slab.reshape(tile_rows, blocks_all, block)]
    all_gather x1 -> x0, local copies, waits for them, and re-layouts: 11.9 us -> none  [body(): column_slab = lax.all_gather(coeff_bf, 'row', axis=0, tiled=True)]
    all_to_all x0 -> x1, starting transfers between devices: none -> 9.19 us  [body(): lax.all_to_all(jnp.stack([coeff_bf for _ in range(lax.axis_size('col'))],...]
    all_gather x1, waiting for transfers between devices: 102 us -> 109 us  [body(): column_slab = lax.all_gather(coeff_bf, 'row', axis=0, tiled=True)]
    another operation x0 -> x1, local copies, waits for them, and re-layouts: none -> 5.07 us  [body(): jnp.stack([coeff_bf for _ in range(lax.axis_size('col'))], axis=0)]
where the time goes in v1:
time: 289 us
  waiting for transfers between devices  232 us (80%)
  local copies, waits for them, and re-layouts  20 us (7%)
  between operations  14.8 us (5%)
  matrix products  10.5 us (4%)
  starting transfers between devices  9.19 us (3%)
    all_to_all x1, waiting for transfers between devices, body(): lax.all_to_all(jnp.stack([coeff_bf for _ in range(lax.axis_size('col'))],...  123 us
    all_gather x1, waiting for transfers between devices, body(): column_slab = lax.all_gather(coeff_bf, 'row', axis=0, tiled=True)  109 us
    all_to_all x1, starting transfers between devices, body(): lax.all_to_all(jnp.stack([coeff_bf for _ in range(lax.axis_size('col'))],...  9.19 us
    gather x1, local copies, waits for them, and re-layouts, body(): beta_picked = slab_cols[:, beta_pattern, :]  7.41 us
    gather x1, local copies, waits for them, and re-layouts, body(): picked = slab_blocks[alpha_pattern]  7.32 us
    dot_general x1, matrix products, body(): jnp.einsum('itab,itbc->iac', weighted, picked, preferred_element_type=jnp...  6.56 us
  transfers between devices with their start and end apart: 2, of which 2 were waited for; matrix products, arithmetic and copies ran while one was open for 4% of the time, Pallas kernels for 0%

profile of v1, /device:TPU:1, one launch (start us, length us, event | category | flops | bytes accessed | tf_op | source)
XLA Modules:
  0.0 288.8 jit_solution(16016620359970388262)
XLA Ops:
  6.5 0.0 all-gather.2.cloned.1.call-start
  6.5 2.1 convert_element_type.22
  8.6 0.0 all-gather.2.cloned.1.call-update
  8.6 5.1 %stack.2 = bf16[16,512,512]{2,1,0:T(8,128)(2,1)} broadcast(bf16[512,512]{1,0:T(8,128)(2,1)} %convert_element_type.22), dimensions={1,2} | broadcast | bytes 8912896 | tf_op jit(solution)/shard_map/stack | solution.py:25
  13.7 0.0 copy-start.1
  13.7 0.0 copy-start.2
  13.7 9.2 %all-to-all-start = ((bf16[16,512,512]{2,1,0:T(8,128)(2,1)}), bf16[16,512,512]{2,1,0:T(8,128)(2,1)}, u32[]{:S(2)}, u32[]{:S(2)}) async-start(bf16[16,512,512]{2,1,0:T(8,128)(2,1)} %stack.2), calls=%async_computation | async-start | bytes 16777216 | tf_op jit(solution)/shard_map/all_to_all | solution.py:24
  24.2 0.0 copy-done.1
  24.3 0.0 copy-done.2
  24.3 109.5 %all-gather.2.cloned.1.call-done = bf16[8192,512]{1,0:T(8,128)(2,1)} async-done(((bf16[512,512]{1,0:T(8,128)(2,1)}), bf16[8192,512]{1,0:T(8,128)(2,1)}) %all-gather.2.cloned.1.call-update) | async-done | bytes 8388624 | tf_op jit(solution)/shard_map/all_gather | solution.py:22
  133.8 7.3 %gather_fusion = bf16[10,512,512]{2,1,0:T(8,128)(2,1)} fusion(bf16[16,512,512]{2,1,0:T(8,128)(2,1)} %bitcast.36, s32[1024]{0:T(1024)S(1)} %pad_clamp_fusion.1), kind=kCustom, calls=%fused_computation | custom fusion | bytes 10485800 | tf_op jit(solution)/shard_map/gather | solution.py:35
  141.1 122.7 %all-to-all-done = bf16[16,512,512]{2,1,0:T(8,128)(2,1)} async-done(((bf16[16,512,512]{2,1,0:T(8,128)(2,1)}), bf16[16,512,512]{2,1,0:T(8,128)(2,1)}, u32[]{:S(2)}, u32[]{:S(2)}) %all-to-all-start) | async-done | bytes 8388640 | tf_op jit(solution)/shard_map/all_to_all | solution.py:24
  263.8 0.0 slice-start
  263.8 7.4 %gather_fusion.1 = bf16[10,512,512]{2,1,0:T(8,128)(2,1)} fusion(bf16[512,16,512]{2,0,1:T(8,128)(2,1)} %bitcast.5, s32[1024]{0:T(1024)S(1)} %pad_clamp_fusion), kind=kCustom, calls=%fused_computation.1 | custom fusion | bytes 10485800 | tf_op jit(solution)/shard_map/gather | solution.py:38
  271.2 0.0 copy-start
  271.2 0.0 slice-start.1
  271.2 6.6 %fusion.9 = f32[512,512]{1,0:T(8,128)S(1)} fusion(bf16[10,512,512]{2,1,0:T(8,128)(2,1)} %gather_fusion, bf16[1,10,512,512]{3,2,1,0:T(8,128)(2,1)} %param.10, bf16[10]{0:T(256)(128)(2,1)S(1)} %compare_convert_fusion.1), kind=kOutput, calls=%fused_computation.11 | convolution fusion | flops 2686976000 | bytes 11534356 | tf_op jit(solution)/shard_map/itab,itbc->iac/dot_general | solution.py:36
  277.8 0.0 slice-done
  277.8 0.0 copy-done
  277.8 0.2 slice-done.1
  278.0 4.0 %fusion.17 = f32[512,512]{1,0:T(8,128)} fusion(f32[512,512]{1,0:T(8,128)S(1)} %fusion.9, bf16[1,10,512,512]{3,2,1,0:T(8,128)(2,1)S(1)} %bitcast.38, bf16[10]{0:T(256)(128)(2,1)S(1)} %compare_convert_fusion, bf16[10,512,512]{2,1,0:T(8,128)(2,1)S(1)} %copy-done), kind=kOutput, calls=%fused_computation.13 | convolution fusion | flops 2687238144 | bytes 12582932 | tf_op jit(solution)/shard_map/abtk,btck->bac/dot_general | solution.py:39
  (7 shorter events, 0.0 us)
Async XLA Ops:
  6.5 127.3 %all-gather.2.cloned.1.call-start = ((), (), s32[]{:S(2)}) async-start(), calls=%async_computation.1 | async-start | bytes 8912896 | tf_op jit(solution)/shard_map/all_gather | solution.py:22
  13.7 10.5 %copy-start.1 = (s32[1,10]{1,0:T(1,128)S(1)}, s32[1,10]{1,0:T(1,128)}, u32[]{:S(2)}) copy-start(s32[1,10]{1,0:T(1,128)} %param.8) | copy-start | bytes 124
  13.7 10.6 %copy-start.2 = (s32[1,10]{1,0:T(1,128)S(1)}, s32[1,10]{1,0:T(1,128)}, u32[]{:S(2)}) copy-start(s32[1,10]{1,0:T(1,128)} %param.11) | copy-start | bytes 124
  13.7 250.1 %all-to-all-start = ((bf16[16,512,512]{2,1,0:T(8,128)(2,1)}), bf16[16,512,512]{2,1,0:T(8,128)(2,1)}, u32[]{:S(2)}, u32[]{:S(2)}) async-start(bf16[16,512,512]{2,1,0:T(8,128)(2,1)} %stack.2), calls=%async_computation | async-start | bytes 16777216 | tf_op jit(solution)/shard_map/all_to_all | solution.py:24
  263.8 14.0 %slice-start = ((s8[5242880]{0:T(1024)(128)(4,1)}), s8[1048576]{0:T(1024)(128)(4,1)S(1)}, s32[]{:S(2)}) async-start(s8[5242880]{0:T(1024)(128)(4,1)} %bitcast.37), calls=%async_computation.2 | async-start | bytes 2097152
  271.2 6.6 %copy-start = (bf16[10,512,512]{2,1,0:T(8,128)(2,1)S(1)}, bf16[10,512,512]{2,1,0:T(8,128)(2,1)}, u32[]{:S(2)}) copy-start(bf16[10,512,512]{2,1,0:T(8,128)(2,1)} %gather_fusion.1) | copy-start | bytes 15728644
  271.2 6.8 %slice-start.1 = ((s8[5242880]{0:T(1024)(128)(4,1)}), s8[4194304]{0:T(1024)(128)(4,1)S(1)}, s32[]{:S(2)}) async-start(s8[5242880]{0:T(1024)(128)(4,1)} %bitcast.37), calls=%async_computation.3 | async-start | bytes 8388608
Sparse Core Ops, SparseCore 0:
  10.1 123.6 all-gather.1
